TPU v7x, 32 devices: a whole 2x2x4 slice. The times are simulated.
32 devices in a mesh: groups: 2 (over y), ctx: 4 (over z), head: 4 (over x, core).
Axes of the slice: x: 2, y: 2, z: 4, core: 2. Of those that a mesh axis runs over, the one named last changes fastest.
Arguments:
- queries: bfloat16 [8192, 512], P(('groups', 'ctx', 'head')), parts along dimension 0, may hold values from -8 to 8, as said below
- keys: bfloat16 [8192, 512], P(('groups', 'ctx', 'head')), parts along dimension 0, may hold values from -8 to 8
- values: bfloat16 [8192, 4096], P(('groups', 'ctx', 'head')), parts along dimension 0, may hold values from -6 to 6
- gain: float32 [4096], P('head'), may hold values from 0.5 to 1.5
Outputs:
- mixed: bfloat16 [8192, 4096], P(('groups', 'ctx', 'head')), parts along dimension 0
There are 2 independent parts, one for each index of `groups`. A program takes and returns all parts, laid end to end along the dimension named above; an argument that names none is the same for every part. Nothing has to cross between parts.
Inputs may be any that keep to these rules, and one draw needn't show every extreme that they name: `queries`: query entries lie in the stated range.
All inputs are finite; a program needn't handle non-finite values.
Results may differ from a plain program's by a relative error of at most 0.0054.
Values may be sent and summed in bfloat16 or wider, within the bound.
No kernel may reach another device: no remote copies, remote signals or barrier semaphores. Data moves between devices by JAX's collectives and lax.ppermute only.
A program may use at most 128 MiB of HBM per device.

v0:
```python
import math
import jax
import jax.numpy as jnp
from jax import lax
from jax.sharding import PartitionSpec as P

HEADS = 32
KD = 16
VD = 128
WINDOW = 64
outer_scale = 1.0 / (4.0 * math.sqrt(2.0))
epsilon = 1e-06


def shifted(shard, axis, by):
    peers = lax.axis_size(axis)
    pairs = [(i, i + by) for i in range(peers) if 0 <= i + by < peers]
    return lax.ppermute(shard, axis, pairs)


def entering(shard, axis, combine, identity):
    peers, here = (lax.axis_size(axis), lax.axis_index(axis))
    everything = lax.all_gather(shard, axis)
    start = jnp.broadcast_to(jnp.asarray(identity, shard.dtype), shard.shape)

    def hop(k, before):
        reached = k < here
        new = combine(before, everything[k])
        return jnp.where(reached, new, before)

    return lax.fori_loop(0, peers, hop, start)


def feature_map(vector):
    width = vector.shape[-1]
    products = (vector[..., :, None] * vector[..., None, :]).reshape(
        vector.shape[:-1] + (width * width,)
    )
    unit_column = jnp.ones(vector.shape[:-1] + (1,), jnp.float32)
    return jnp.concatenate([unit_column, vector * 0.5, products * outer_scale], axis=-1)


def per_device(queries, keys, values, gain):
    local_tokens = queries.shape[0]
    query_tok = queries.reshape(local_tokens, HEADS, KD)
    key_tok = keys.reshape(local_tokens, HEADS, KD)
    value_tok = values.reshape(local_tokens, HEADS, VD)
    query_head, key_head, value_head = (
        lax.all_to_all(query_tok, "head", split_axis=1, concat_axis=0, tiled=True),
        lax.all_to_all(key_tok, "head", split_axis=1, concat_axis=0, tiled=True),
        lax.all_to_all(value_tok, "head", split_axis=1, concat_axis=0, tiled=True),
    )
    span_rows = query_head.shape[0]
    heads_here = query_head.shape[1]
    block_rows = min(512, span_rows)
    block_count = span_rows // block_rows
    tail_keys, tail_values = shifted(
        (key_head[span_rows - WINDOW :], value_head[span_rows - WINDOW :]), "ctx", 1
    )
    key_ext = jnp.concatenate([tail_keys, key_head], axis=0)
    value_ext = jnp.concatenate([tail_values, value_head], axis=0)
    first_span = lax.axis_index("ctx") == 0
    key_features = feature_map(key_head.astype(jnp.float32)).astype(jnp.bfloat16)
    own_state = jnp.einsum(
        "bhf,bhv->hfv", key_features, value_head, preferred_element_type=jnp.float32
    )

    def combine_states(earlier, later):
        return earlier + later

    prefix = entering(own_state, "ctx", combine_states, jnp.zeros_like(own_state))

    def block_step(state, block_index):
        start = block_index * block_rows
        query_block = lax.dynamic_slice_in_dim(query_head, start, block_rows, 0)
        key_block = lax.dynamic_slice_in_dim(key_head, start, block_rows, 0)
        value_block = lax.dynamic_slice_in_dim(value_head, start, block_rows, 0)
        key_feat = lax.dynamic_slice_in_dim(key_features, start, block_rows, 0)
        key_window = lax.dynamic_slice_in_dim(key_ext, start, block_rows + WINDOW, 0)
        value_window = lax.dynamic_slice_in_dim(value_ext, start, block_rows + WINDOW, 0)
        scores = (
            jnp.einsum("bhd,chd->hbc", query_block, key_block, preferred_element_type=jnp.float32)
            * 0.25
        )
        row_pos = jnp.arange(block_rows)[:, None]
        col_pos = jnp.arange(block_rows)[None, :]
        kernel = jnp.where(col_pos <= row_pos, 1.0 + scores + 0.5 * scores * scores, 0.0).astype(
            jnp.bfloat16
        )
        intra = jnp.einsum("hbc,chv->bhv", kernel, value_block, preferred_element_type=jnp.float32)
        query_feat = feature_map(query_block.astype(jnp.float32)).astype(jnp.bfloat16)
        inter = jnp.einsum(
            "bhf,hfv->bhv",
            query_feat,
            state.astype(jnp.bfloat16),
            preferred_element_type=jnp.float32,
        )
        state = state + jnp.einsum(
            "bhf,bhv->hfv", key_feat, value_block, preferred_element_type=jnp.float32
        )
        window_scores = (
            jnp.einsum("bhd,chd->hbc", query_block, key_window, preferred_element_type=jnp.float32)
            * 0.25
        )
        key_pos = jnp.arange(block_rows + WINDOW)[None, :] - WINDOW
        valid = (
            (key_pos <= row_pos)
            & (key_pos > row_pos - WINDOW)
            & ((start + key_pos >= 0) | jnp.logical_not(first_span))
        )
        masked = jnp.where(valid, window_scores, -jnp.inf)
        highest_score = jnp.max(masked, axis=2, keepdims=True)
        expo = jnp.where(valid, jnp.exp(window_scores - highest_score), 0.0)
        weights = (expo / jnp.sum(expo, axis=2, keepdims=True)).astype(jnp.bfloat16)
        window_out = jnp.einsum(
            "hbc,chv->bhv", weights, value_window, preferred_element_type=jnp.float32
        )
        return (state, (intra + inter, window_out))

    final_state, (linear_all, window_all) = lax.scan(block_step, prefix, jnp.arange(block_count))
    linear = linear_all.reshape(span_rows, heads_here, VD)
    window = window_all.reshape(span_rows, heads_here, VD)
    scale = lax.rsqrt(jnp.mean(linear * linear, axis=2, keepdims=True) + epsilon)
    gains = gain.reshape(heads_here, VD)
    mixed = (linear * scale * gains + window).astype(jnp.bfloat16)
    tokens_back = lax.all_to_all(mixed, "head", split_axis=0, concat_axis=1, tiled=True)
    return tokens_back.reshape(tokens_back.shape[0], HEADS * VD)


def solution(mesh):
    placed = (
        P(("groups", "ctx", "head"), None),
        P(("groups", "ctx", "head"), None),
        P(("groups", "ctx", "head"), None),
        P("head"),
    )
    return jax.shard_map(
        per_device,
        mesh=mesh,
        in_specs=placed,
        out_specs=P(("groups", "ctx", "head"), None),
        check_vma=False,
    )
```

profile of v0, /device:TPU:0, one launch (start us, length us, event | category | flops | bytes accessed | tf_op | source)
XLA Modules:
  0.0 278.9 jit_solution(16457745592861958230)
XLA Ops:
  6.5 1.8 copy.42
  8.3 4.2 %all-to-all-start = ((bf16[256,32,16]{0,2,1:T(8,128)(2,1)}), bf16[256,32,16]{0,2,1:T(8,128)(2,1)S(1)}, u32[]{:S(2)}, u32[]{:S(2)}) async-start(bf16[256,32,16]{0,2,1:T(8,128)(2,1)} %bitcast.7), calls=%async_computation | async-start | bytes 524288 | tf_op jit(solution)/shard_map/all_to_all | solution.py:50
  12.5 3.3 %copy.44 = bf16[256,4096]{0,1:T(8,128)(2,1)S(1)} copy(bf16[256,4096]{1,0:T(8,128)(2,1)} %param.10) | data formatting | bytes 4194304 | tf_op args[2]
  15.8 2.9 %copy.45 = bf16[256,32,128]{2,0,1:T(8,128)(2,1)} copy(bf16[256,32,128]{0,2,1:T(8,128)(2,1)S(1)} %bitcast.80) | data formatting | bytes 4194304 | tf_op jit(solution)/shard_map/reshape | solution.py:47
  18.7 3.6 %all-to-all-start.1 = ((bf16[256,32,128]{2,0,1:T(8,128)(2,1)}), bf16[256,32,128]{2,0,1:T(8,128)(2,1)S(1)}, u32[]{:S(2)}, u32[]{:S(2)}) async-start(bf16[256,32,128]{2,0,1:T(8,128)(2,1)} %copy.45), calls=%async_computation.1 | async-start | bytes 4194304 | tf_op jit(solution)/shard_map/all_to_all | solution.py:51
  22.5 1.3 multiply_convert_fusion.2
  23.8 3.9 %pad_maximum_fusion = bf16[1024,8,273]{0,2,1:T(8,128)(2,1)} fusion(bf16[1024,8,256]{0,2,1:T(8,128)(2,1)S(1)} %bitcast.76, bf16[1024,8,16]{0,2,1:T(8,128)(2,1)S(1)} %multiply_convert_fusion.3, bf16[273]{0:T(512)(128)(2,1)S(1)} %pad.7.clone), kind=kLoop, calls=%fused_computation.66 | loop fusion | flops 13418496 | bytes 8929826 | tf_op jit(solution)/shard_map/concatenate | solution.py:40
  27.7 20.3 %all-to-all-done.1 = bf16[256,32,128]{2,0,1:T(8,128)(2,1)S(1)} async-done(((bf16[256,32,128]{2,0,1:T(8,128)(2,1)}), bf16[256,32,128]{2,0,1:T(8,128)(2,1)S(1)}, u32[]{:S(2)}, u32[]{:S(2)}) %all-to-all-start.1) | async-done | bytes 2097184 | tf_op jit(solution)/shard_map/all_to_all | solution.py:51
  48.0 1.5 copy.47
  49.4 4.4 %fusion.77 = f32[8,273,128]{2,1,0:T(8,128)S(1)} fusion(bf16[1024,8,273]{0,2,1:T(8,128)(2,1)} %pad_maximum_fusion, bf16[1024,8,128]{2,0,1:T(8,128)(2,1)} %bitcast.15), kind=kOutput, calls=%fused_computation.77 | convolution fusion | flops 572522496 | bytes 7688192 | tf_op jit(solution)/shard_map/bhf,bhv->hfv/dot_general | solution.py:64
  53.8 1.3 copy.48
  55.1 0.8 copy.50
  55.9 3.4 %all-to-all-start.2 = ((bf16[256,32,16]{0,2,1:T(8,128)(2,1)}), bf16[256,32,16]{0,2,1:T(8,128)(2,1)S(1)}, u32[]{:S(2)}, u32[]{:S(2)}) async-start(bf16[256,32,16]{0,2,1:T(8,128)(2,1)} %bitcast.17), calls=%async_computation.2 | async-start | bytes 524288 | tf_op jit(solution)/shard_map/all_to_all | solution.py:49
  59.4 4.1 %collective-permute-start.1 = (bf16[64,8,16]{0,2,1:T(8,128)(2,1)S(1)}, bf16[64,8,16]{0,2,1:T(8,128)(2,1)S(1)}, u32[]{:S(2)}, u32[]{:S(2)}) collective-permute-start(bf16[64,8,16]{0,2,1:T(8,128)(2,1)S(1)} %slice.9), channel_id=1, source_target_pairs={{0,4},{4,8},{8,12},{1,5},{5,9},{9,13},{2,6},{6,10},{10,14},{3,7},{... | collective-permute-start | bytes 49160 | tf_op jit(solution)/shard_map/ppermute | solution.py:18
  63.6 1.7 all-to-all-done.2
  65.3 0.8 copy.65
  66.1 0.9 slice.8
  67.0 4.3 %collective-permute-start = (bf16[64,8,128]{2,0,1:T(8,128)(2,1)S(1)}, bf16[64,8,128]{2,0,1:T(8,128)(2,1)S(1)}, u32[]{:S(2)}, u32[]{:S(2)}) collective-permute-start(bf16[64,8,128]{2,0,1:T(8,128)(2,1)S(1)} %slice.8), channel_id=1, source_target_pairs={{0,4},{4,8},{8,12},{1,5},{5,9},{9,13},{2,6},{6,10},{10,14},{3,7},{... | collective-permute-start | bytes 393224 | tf_op jit(solution)/shard_map/ppermute | solution.py:18
  71.4 0.9 pad_maximum_fusion.2
  72.2 5.1 %collective-permute-done = bf16[64,8,128]{2,0,1:T(8,128)(2,1)S(1)} collective-permute-done((bf16[64,8,128]{2,0,1:T(8,128)(2,1)S(1)}, bf16[64,8,128]{2,0,1:T(8,128)(2,1)S(1)}, u32[]{:S(2)}, u32[]{:S(2)}) %collective-permute-start) | collective-permute-done | bytes 131104 | tf_op jit(solution)/shard_map/ppermute | solution.py:18
  77.4 3.1 %pad_maximum_fusion.1 = bf16[1088,8,128]{2,0,1:T(8,128)(2,1)} fusion(bf16[1024,8,128]{2,0,1:T(8,128)(2,1)} %bitcast.15, bf16[64,8,128]{2,0,1:T(8,128)(2,1)S(1)} %collective-permute-done), kind=kLoop, calls=%fused_computation.72 | loop fusion | flops 4456448 | bytes 4456448 | tf_op jit(solution)/shard_map/concatenate | solution.py:61
  80.5 65.2 %all-gather.3.cloned.1.call-done = f32[32,273,128]{2,0,1:T(8,128)} async-done(((f32[8,273,128]{2,0,1:T(8,128)}), f32[32,273,128]{2,0,1:T(8,128)}) %all-gather.3.cloned.1.call-update) | async-done | bytes 4472848 | tf_op jit(solution)/shard_map/all_gather | solution.py:23
  145.7 7.5 %while.32 = (s32[]{:T(128)}, f32[8,273,128]{2,1,0:T(8,128)S(1)}, s32[]{:T(128)}, f32[4,8,273,128]{3,1,0,2:T(8,128)}, s32[]{:T(128)}, /*index=5*/s32[]{:T(128)}) while((s32[]{:T(128)}, f32[8,273,128]{2,1,0:T(8,128)S(1)}, s32[]{:T(128)}, f32[4,8,273,128]{3,1,0,2:T(8,128)}, s32[]{:T(128)}, /*index=5*/s32[]{:T(128)}) %tuple.69), condition=%wide.region_1.2_spmd.clone, body=%wide.region_0.1_spmd.clone.sunk | while | flops 838660 | bytes 5591141 | solution.py:31
  145.7 1.3 constant_dynamic-slice_fusion.2
  147.0 0.5 add_select_fusion.2
  147.6 1.3 constant_dynamic-slice_fusion.2
  148.9 0.5 add_select_fusion.2
  149.5 1.3 constant_dynamic-slice_fusion.2
  150.8 0.5 add_select_fusion.2
  151.4 1.3 constant_dynamic-slice_fusion.2
  152.7 0.5 add_select_fusion.2
  153.2 71.0 %while.31 = (s32[]{:T(128)}, f32[8,273,128]{2,1,0:T(8,128)S(1)}, f32[2,512,8,128]{1,3,2,0:T(8,128)}, f32[2,512,8,128]{3,2,1,0:T(8,128)}, s32[2]{0:T(128)S(1)}, /...) while((s32[]{:T(128)}, f32[8,273,128]{2,1,0:T(8,128)S(1)}, ...), condition=%wide.region_5.6_spmd, body=%wide.region_2.5_spmd.sunk | while | flops 1977677568 | bytes 70311560 | solution.py:120
  153.3 0.6 dynamic_slice.126
  154.5 1.6 multiply_convert_fusion.7
  156.1 0.9 dynamic-slice_convert_fusion.2
  157.0 0.8 iota_compare_fusion.3
  157.9 1.1 fusion.113
  158.9 4.5 %fusion.111 = f32[8,128,512]{2,1,0:T(8,128)S(1)} fusion(pred[512,512]{1,0:T(8,128)(4,1)} %iota_compare_fusion.3, bf16[1024,8,128]{2,0,1:T(8,128)(2,1)} %get-tuple-element.495, s32[]{:T(128)S(6)} %select_n.84, bf16[1024,8,16]{0,2,1:T(8,128)(2,1)} %copy-done.1, bf16[1024,8,16]{0,2,1:T(8,128)(2,1)} %get-tuple-element.496), kind=kOutput, calls=%fused_computation.12.clone.1 | convolution fusion | flops 618659840 | bytes 3671552 | tf_op jit(solution)/shard_map/while/body/eval_jaxpr/hbc,chv->bhv/dot_general | solution.py:90
  163.5 0.7 multiply_convert_fusion.6
  164.2 3.7 %bitcast_dynamic-update-slice_fusion.2 = f32[2,512,8,128]{1,3,2,0:T(8,128)} fusion(f32[2,512,8,128]{1,3,2,0:T(8,128)} %get-tuple-element.472, s32[]{:T(128)S(6)} %copy.85, f32[8,128,512]{2,1,0:T(8,128)S(1)} %fusion.111, bf16[512,8,256]{0,2,1:T(8,128)(2,1)S(1)} %bitcast.73, bf16[512,8,16]{0,2,1:T(8,128)(2,1)} %multiply_convert_fusion.7, ...), kind=kOutput, calls=%fused_computation.22.clone.1 | convolution fusion | flops 293774336 | bytes 7541286 | tf_op jit(solution)/shard_map/while/body/eval_jaxpr/bhf,hfv->bhv/dot_general | solution.py:92
  167.9 2.3 fusion.110
  170.2 8.4 %fusion.114 = (f32[8,512]{1,0:T(8,128)S(1)}, f32[8,512,576]{1,2,0:T(8,128)}) fusion(pred[512,576]{0,1:T(8,128)(4,1)S(1)} %copy-done, bf16[1088,8,16]{0,2,1:T(8,128)(2,1)S(1)} %copy-done.3, s32[]{:T(128)S(6)} %select_n.85, bf16[1024,8,16]{0,2,1:T(8,128)(2,1)} %get-tuple-element.496, s32[]{:T(128)S(6)} %select_n.84), kind=kOutput, calls=%fused_computation.76.clone.1 | convolution fusion | flops 165151296 | bytes 10635264 | tf_op jit(solution)/shard_map/while/body/eval_jaxpr/sub | solution.py:113
  178.6 6.5 %fusion.115 = f32[1,512,8,128]{1,3,2,0:T(8,128)} fusion(f32[8,512,576]{1,2,0:T(8,128)} %get-tuple-element.427, f32[8,512]{1,0:T(8,128)S(1)} %get-tuple-element.428, bf16[1088,8,128]{2,0,1:T(8,128)(2,1)} %get-tuple-element.498, s32[]{:T(128)S(6)} %select_n.85), kind=kOutput, calls=%fused_computation.24.clone.1 | convolution fusion | flops 608698368 | bytes 12730372 | tf_op jit(solution)/shard_map/while/body/eval_jaxpr/hbc,chv->bhv/dot_general | solution.py:115
  185.1 2.1 copy.71
  187.2 1.5 constant_dynamic-update-slice_fusion.2
  188.7 0.7 dynamic_slice.126
  190.0 1.6 multiply_convert_fusion.7
  191.6 0.9 dynamic-slice_convert_fusion.2
  192.5 0.8 iota_compare_fusion.3
  193.3 1.1 fusion.113
  194.4 4.6 %fusion.111 = f32[8,128,512]{2,1,0:T(8,128)S(1)} fusion(pred[512,512]{1,0:T(8,128)(4,1)} %iota_compare_fusion.3, bf16[1024,8,128]{2,0,1:T(8,128)(2,1)} %get-tuple-element.495, s32[]{:T(128)S(6)} %select_n.84, bf16[1024,8,16]{0,2,1:T(8,128)(2,1)} %copy-done.1, bf16[1024,8,16]{0,2,1:T(8,128)(2,1)} %get-tuple-element.496), kind=kOutput, calls=%fused_computation.12.clone.1 | convolution fusion | flops 618659840 | bytes 3671552 | tf_op jit(solution)/shard_map/while/body/eval_jaxpr/hbc,chv->bhv/dot_general | solution.py:90
  199.0 0.7 multiply_convert_fusion.6
  199.6 3.7 %bitcast_dynamic-update-slice_fusion.2 = f32[2,512,8,128]{1,3,2,0:T(8,128)} fusion(f32[2,512,8,128]{1,3,2,0:T(8,128)} %get-tuple-element.472, s32[]{:T(128)S(6)} %copy.85, f32[8,128,512]{2,1,0:T(8,128)S(1)} %fusion.111, bf16[512,8,256]{0,2,1:T(8,128)(2,1)S(1)} %bitcast.73, bf16[512,8,16]{0,2,1:T(8,128)(2,1)} %multiply_convert_fusion.7, ...), kind=kOutput, calls=%fused_computation.22.clone.1 | convolution fusion | flops 293774336 | bytes 7541286 | tf_op jit(solution)/shard_map/while/body/eval_jaxpr/bhf,hfv->bhv/dot_general | solution.py:92
  203.4 2.3 fusion.110
  205.7 8.4 %fusion.114 = (f32[8,512]{1,0:T(8,128)S(1)}, f32[8,512,576]{1,2,0:T(8,128)}) fusion(pred[512,576]{0,1:T(8,128)(4,1)S(1)} %copy-done, bf16[1088,8,16]{0,2,1:T(8,128)(2,1)S(1)} %copy-done.3, s32[]{:T(128)S(6)} %select_n.85, bf16[1024,8,16]{0,2,1:T(8,128)(2,1)} %get-tuple-element.496, s32[]{:T(128)S(6)} %select_n.84), kind=kOutput, calls=%fused_computation.76.clone.1 | convolution fusion | flops 165151296 | bytes 10635264 | tf_op jit(solution)/shard_map/while/body/eval_jaxpr/sub | solution.py:113
  214.1 6.5 %fusion.115 = f32[1,512,8,128]{1,3,2,0:T(8,128)} fusion(f32[8,512,576]{1,2,0:T(8,128)} %get-tuple-element.427, f32[8,512]{1,0:T(8,128)S(1)} %get-tuple-element.428, bf16[1088,8,128]{2,0,1:T(8,128)(2,1)} %get-tuple-element.498, s32[]{:T(128)S(6)} %select_n.85), kind=kOutput, calls=%fused_computation.24.clone.1 | convolution fusion | flops 608698368 | bytes 12730372 | tf_op jit(solution)/shard_map/while/body/eval_jaxpr/hbc,chv->bhv/dot_general | solution.py:115
  220.6 2.1 copy.71
  222.7 1.5 constant_dynamic-update-slice_fusion.2
  224.2 2.8 multiply_reduce_fusion
  227.0 5.3 %copy.52 = f32[2,512,8,128]{3,2,1,0:T(8,128)} copy(f32[2,512,8,128]{1,3,2,0:T(8,128)} %get-tuple-element.272) | data formatting | bytes 8388608 | tf_op jit(solution)/shard_map/while | solution.py:120
  232.5 4.1 %fusion.66 = bf16[1024,8,128]{2,1,0:T(8,128)(2,1)S(1)} fusion(f32[2,512,8,128]{3,2,1,0:T(8,128)} %get-tuple-element.273, f32[2,512,8,128]{3,2,1,0:T(8,128)} %copy.52, f32[8,128]{1,0:T(8,128)S(1)} %bitcast.90, f32[1024,8]{1,0:T(8,128)S(1)} %copy.53), kind=kLoop, calls=%fused_computation.68 | loop fusion | flops 4194304 | bytes 10522624 | tf_op jit(solution)/shard_map/convert_element_type | solution.py:125
  236.6 28.8 %all_to_all.69 = bf16[1024,8,128]{2,1,0:T(8,128)(2,1)S(1)} all-to-all(bf16[1024,8,128]{2,1,0:T(8,128)(2,1)S(1)} %fusion.66), channel_id=1, replica_groups=mesh['groups'=2,'ctx'=4,'head'=4] {'head'}, dimensions={0} | all-to-all | bytes 4194304 | tf_op jit(solution)/shard_map/all_to_all | solution.py:126
  265.4 2.6 copy.55
  268.0 4.1 %copy.56 = bf16[256,4096]{1,0:T(8,128)(2,1)} copy(bf16[256,4096]{0,1:T(8,128)(2,1)} %bitcast.79) | data formatting | bytes 4194304 | tf_op jit(solution)/shard_map/reshape | solution.py:127
  (53 shorter events, 0.6 us)
Async XLA Ops:
  8.3 10.3 %all-to-all-start = ((bf16[256,32,16]{0,2,1:T(8,128)(2,1)}), bf16[256,32,16]{0,2,1:T(8,128)(2,1)S(1)}, u32[]{:S(2)}, u32[]{:S(2)}) async-start(bf16[256,32,16]{0,2,1:T(8,128)(2,1)} %bitcast.7), calls=%async_computation | async-start | bytes 524288 | tf_op jit(solution)/shard_map/all_to_all | solution.py:50
  18.7 29.3 %all-to-all-start.1 = ((bf16[256,32,128]{2,0,1:T(8,128)(2,1)}), bf16[256,32,128]{2,0,1:T(8,128)(2,1)S(1)}, u32[]{:S(2)}, u32[]{:S(2)}) async-start(bf16[256,32,128]{2,0,1:T(8,128)(2,1)} %copy.45), calls=%async_computation.1 | async-start | bytes 4194304 | tf_op jit(solution)/shard_map/all_to_all | solution.py:51
  22.3 123.4 %all-gather.3.cloned.1.call-start = ((), (), s32[]{:S(2)}) async-start(), calls=%async_computation.4 | async-start | bytes 5591040 | tf_op jit(solution)/shard_map/all_gather | solution.py:23
  49.4 5.7 %copy-start.4 = (bf16[256,512]{1,0:T(8,128)(2,1)S(1)}, bf16[256,512]{1,0:T(8,128)(2,1)}, u32[]{:S(2)}) copy-start(bf16[256,512]{1,0:T(8,128)(2,1)} %param.8) | copy-start | bytes 786436
  55.9 9.4 %all-to-all-start.2 = ((bf16[256,32,16]{0,2,1:T(8,128)(2,1)}), bf16[256,32,16]{0,2,1:T(8,128)(2,1)S(1)}, u32[]{:S(2)}, u32[]{:S(2)}) async-start(bf16[256,32,16]{0,2,1:T(8,128)(2,1)} %bitcast.17), calls=%async_computation.2 | async-start | bytes 524288 | tf_op jit(solution)/shard_map/all_to_all | solution.py:49
  59.4 11.9 %collective-permute-start.1 = (bf16[64,8,16]{0,2,1:T(8,128)(2,1)S(1)}, bf16[64,8,16]{0,2,1:T(8,128)(2,1)S(1)}, u32[]{:S(2)}, u32[]{:S(2)}) collective-permute-start(bf16[64,8,16]{0,2,1:T(8,128)(2,1)S(1)} %slice.9), channel_id=1, source_target_pairs={{0,4},{4,8},{8,12},{1,5},{5,9},{9,13},{2,6},{6,10},{10,14},{3,7},{... | collective-permute-start | bytes 49160 | tf_op jit(solution)/shard_map/ppermute | solution.py:18
  67.0 10.3 %collective-permute-start = (bf16[64,8,128]{2,0,1:T(8,128)(2,1)S(1)}, bf16[64,8,128]{2,0,1:T(8,128)(2,1)S(1)}, u32[]{:S(2)}, u32[]{:S(2)}) collective-permute-start(bf16[64,8,128]{2,0,1:T(8,128)(2,1)S(1)} %slice.8), channel_id=1, source_target_pairs={{0,4},{4,8},{8,12},{1,5},{5,9},{9,13},{2,6},{6,10},{10,14},{3,7},{... | collective-permute-start | bytes 393224 | tf_op jit(solution)/shard_map/ppermute | solution.py:18
  153.2 4.6 %copy-start.1 = (bf16[1024,8,16]{0,2,1:T(8,128)(2,1)}, bf16[1024,8,16]{0,2,1:T(8,128)(2,1)S(1)}, u32[]{:S(2)}) copy-start(bf16[1024,8,16]{0,2,1:T(8,128)(2,1)S(1)} %get-tuple-element.497) | copy-start | bytes 786436 | tf_op jit(solution)/shard_map/while
  163.5 4.4 %slice-start = ((s8[4587520]{0:T(1024)(128)(4,1)}), s8[4194304]{0:T(1024)(128)(4,1)S(1)}, s32[]{:S(2)}) async-start(s8[4587520]{0:T(1024)(128)(4,1)} %bitcast.74), calls=%async_computation.5 | async-start | bytes 8388608 | tf_op jit(solution)/shard_map/while
  164.2 3.7 %slice-start.1 = ((s8[4587520]{0:T(1024)(128)(4,1)}), s8[393216]{0:T(1024)(128)(4,1)S(1)}, s32[]{:S(2)}) async-start(s8[4587520]{0:T(1024)(128)(4,1)} %bitcast.74), calls=%async_computation.6 | async-start | bytes 786432 | tf_op jit(solution)/shard_map/while
  167.9 2.3 copy-start
  167.9 2.3 copy-start.3
  185.1 3.6 %copy-start.2 = (bf16[1024,8,16]{0,2,1:T(8,128)(2,1)S(1)}, bf16[1024,8,16]{0,2,1:T(8,128)(2,1)}, u32[]{:S(2)}) copy-start(bf16[1024,8,16]{0,2,1:T(8,128)(2,1)} %copy-done.1) | copy-start | bytes 786436 | tf_op jit(solution)/shard_map/while
  188.7 4.6 %copy-start.1 = (bf16[1024,8,16]{0,2,1:T(8,128)(2,1)}, bf16[1024,8,16]{0,2,1:T(8,128)(2,1)S(1)}, u32[]{:S(2)}) copy-start(bf16[1024,8,16]{0,2,1:T(8,128)(2,1)S(1)} %get-tuple-element.497) | copy-start | bytes 786436 | tf_op jit(solution)/shard_map/while
  198.9 4.4 %slice-start = ((s8[4587520]{0:T(1024)(128)(4,1)}), s8[4194304]{0:T(1024)(128)(4,1)S(1)}, s32[]{:S(2)}) async-start(s8[4587520]{0:T(1024)(128)(4,1)} %bitcast.74), calls=%async_computation.5 | async-start | bytes 8388608 | tf_op jit(solution)/shard_map/while
  199.6 3.7 %slice-start.1 = ((s8[4587520]{0:T(1024)(128)(4,1)}), s8[393216]{0:T(1024)(128)(4,1)S(1)}, s32[]{:S(2)}) async-start(s8[4587520]{0:T(1024)(128)(4,1)} %bitcast.74), calls=%async_computation.6 | async-start | bytes 786432 | tf_op jit(solution)/shard_map/while
  203.4 2.4 copy-start
  203.4 2.4 copy-start.3
  220.6 3.6 %copy-start.2 = (bf16[1024,8,16]{0,2,1:T(8,128)(2,1)S(1)}, bf16[1024,8,16]{0,2,1:T(8,128)(2,1)}, u32[]{:S(2)}) copy-start(bf16[1024,8,16]{0,2,1:T(8,128)(2,1)} %copy-done.1) | copy-start | bytes 786436 | tf_op jit(solution)/shard_map/while
  227.0 5.5 %copy-start.5 = (f32[1024]{0:T(1024)S(1)}, f32[1024]{0:T(1024)}, u32[]{:S(2)}) copy-start(f32[1024]{0:T(1024)} %param.11) | copy-start | bytes 12292
Sparse Core Ops, SparseCore 0:
  55.2 90.4 all-gather.2
where the time goes:
time: 280 us; the launch traced here: 279 us
  waiting for transfers between devices  92.4 us (33%)
  matrix products  55.3 us (20%)
  local copies, waits for them, and re-layouts  39.3 us (14%)
  blocking collectives  28.8 us (10%)
  other arithmetic  28.4 us (10%)
  starting transfers between devices  19.7 us (7%)
  between operations  13.6 us (5%)
    all_gather x1, waiting for transfers between devices, entering(): everything = lax.all_gather(shard, axis)  65.2 us
    all_to_all x1, blocking collectives, per_device(): lax.all_to_all(mixed, 'head', split_axis=0, concat_axis=1, tiled=True)  28.8 us
    all_to_all x1, waiting for transfers between devices, per_device(): lax.all_to_all(value_tok, 'head', split_axis=1, concat_axis=0, tiled=True)  20.3 us
    sub x2, matrix products, block_step(): expo = jnp.where(valid, jnp.exp(window_scores - highest_score), 0.0)  16.7 us
    dot_general x2, matrix products, block_step(): jnp.einsum('hbc,chv->bhv', weights, value_window, preferred_element_type=...  13 us
    dot_general x2, matrix products, block_step(): jnp.einsum('hbc,chv->bhv', kernel, value_block, preferred_element_type=jn...  9.1 us
    ppermute x2, starting transfers between devices, shifted(): return lax.ppermute(shard, axis, pairs)  8.46 us
    dot_general x2, matrix products, block_step(): jnp.einsum('bhf,hfv->bhv', query_feat, state.astype(jnp.bfloat16), prefer...  7.45 us
  transfers between devices with their start and end apart: 6, of which 4 were waited for; matrix products, arithmetic and copies ran while one was open for 6% of the time, Pallas kernels for 0%

commit v1 on v0

--- a/solution.py
+++ b/solution.py
@@ -10,6 +10,17 @@
 WINDOW = 64
 outer_scale = 1.0 / (4.0 * math.sqrt(2.0))
 epsilon = 1e-06
+
+
+def split_up(x, dim, devices):
+    before, after = (x.shape[:dim], x.shape[dim + 1 :])
+    return jnp.moveaxis(x.reshape(*before, devices, -1, *after), dim, 0)
+
+
+def joined_along(pieces, dim):
+    shape = list(pieces.shape[1:])
+    shape[dim] *= pieces.shape[0]
+    return jnp.moveaxis(pieces, 0, dim).reshape(shape)
 
 
 def shifted(shard, axis, by):
@@ -123,7 +134,16 @@
     scale = lax.rsqrt(jnp.mean(linear * linear, axis=2, keepdims=True) + epsilon)
     gains = gain.reshape(heads_here, VD)
     mixed = (linear * scale * gains + window).astype(jnp.bfloat16)
-    tokens_back = lax.all_to_all(mixed, "head", split_axis=0, concat_axis=1, tiled=True)
+    length, index = (lax.axis_size("head"), lax.axis_index("head"))
+    blocks = split_up(mixed, 0, length)
+    outs = [blocks[index]]
+    for step in range(1, length):
+        sent = blocks[(index + step) % length]
+        outs.append(
+            lax.ppermute(sent, "head", [(i_2, (i_2 + step) % length) for i_2 in range(length)])
+        )
+    blocks = jnp.stack(outs)[(index - jnp.arange(length)) % length]
+    tokens_back = joined_along(blocks, 1)
     return tokens_back.reshape(tokens_back.shape[0], HEADS * VD)
 
 

time: 280 us -> 268 us (0.957)
  blocking collectives: 28.8 us -> 0 us
  waiting for transfers between devices: 92.4 us -> 117 us
  matrix products: 55.3 us -> 48.4 us
  other arithmetic: 28.4 us -> 21.7 us
  local copies, waits for them, and re-layouts: 39.3 us -> 42.8 us
    all_to_all x1 -> x0, blocking collectives: 28.8 us -> none  [per_device(): lax.all_to_all(mixed, 'head', split_axis=0, concat_axis=1, tiled=True)]
    ppermute x0 -> x3, waiting for transfers between devices: none -> 23.7 us  [per_device(): lax.ppermute(sent, 'head', [(i_2, (i_2 + step) % length) for i_2 in range...]
    reshape x1 -> x0, local copies, waits for them, and re-layouts: 4.06 us -> none  [per_device(): return tokens_back.reshape(tokens_back.shape[0], HEADS * VD)]
    transpose x0 -> x1, local copies, waits for them, and re-layouts: none -> 2.99 us  [joined_along(): return jnp.moveaxis(pieces, 0, dim).reshape(shape)]
    another operation x0 -> x1, local copies, waits for them, and re-layouts: none -> 2.86 us  [per_device(): return tokens_back.reshape(tokens_back.shape[0], HEADS * VD)]
    another operation x8 -> x9, other arithmetic: 5.83 us -> 2.99 us
    unnamed x7 -> x15, local copies, waits for them, and re-layouts: 5.9 us -> 7.95 us
  transfers between devices with their start and end apart: 6 -> 9, of which waited for: 4 -> 6; matrix products, arithmetic and copies ran while one was open for 6% -> 6% of each run, Pallas kernels for 0% -> 0%
where the time goes in v1:
time: 268 us; the launch traced here: 267 us
  waiting for transfers between devices  117 us (44%)
  matrix products  48.4 us (18%)
  local copies, waits for them, and re-layouts  42.8 us (16%)
  starting transfers between devices  21.7 us (8%)
  other arithmetic  21.7 us (8%)
  between operations  13.7 us (5%)
    all_gather x1, waiting for transfers between devices, entering(): everything = lax.all_gather(shard, axis)  67.5 us
    ppermute x3, waiting for transfers between devices, per_device(): lax.ppermute(sent, 'head', [(i_2, (i_2 + step) % length) for i_2 in range...  23.7 us
    all_to_all x1, waiting for transfers between devices, per_device(): lax.all_to_all(value_tok, 'head', split_axis=1, concat_axis=0, tiled=True)  20.3 us
    sub x2, matrix products, block_step(): expo = jnp.where(valid, jnp.exp(window_scores - highest_score), 0.0)  14.9 us
    dot_general x2, matrix products, block_step(): jnp.einsum('hbc,chv->bhv', weights, value_window, preferred_element_type=...  13 us
    dot_general x2, matrix products, block_step(): jnp.einsum('hbc,chv->bhv', kernel, value_block, preferred_element_type=jn...  9.04 us
    ppermute x2, starting transfers between devices, shifted(): return lax.ppermute(shard, axis, pairs)  8.45 us
    unnamed x15, local copies, waits for them, and re-layouts  7.95 us
  transfers between devices with their start and end apart: 9, of which 6 were waited for; matrix products, arithmetic and copies ran while one was open for 6% of the time, Pallas kernels for 0%

profile of v1, /device:TPU:0, one launch (start us, length us, event | category | flops | bytes accessed | tf_op | source)
XLA Modules:
  0.0 266.7 jit_solution(3608715375270540987)
XLA Ops:
  6.5 1.8 copy.42
  8.3 4.2 %all-to-all-start = ((bf16[256,32,16]{0,2,1:T(8,128)(2,1)}), bf16[256,32,16]{0,2,1:T(8,128)(2,1)S(1)}, u32[]{:S(2)}, u32[]{:S(2)}) async-start(bf16[256,32,16]{0,2,1:T(8,128)(2,1)} %bitcast.7), calls=%async_computation | async-start | bytes 524288 | tf_op jit(solution)/shard_map/all_to_all | solution.py:61
  12.5 3.3 %copy.44 = bf16[256,4096]{0,1:T(8,128)(2,1)S(1)} copy(bf16[256,4096]{1,0:T(8,128)(2,1)} %param.10) | data formatting | bytes 4194304 | tf_op args[2]
  15.8 2.9 %copy.45 = bf16[256,32,128]{2,0,1:T(8,128)(2,1)} copy(bf16[256,32,128]{0,2,1:T(8,128)(2,1)S(1)} %bitcast.87) | data formatting | bytes 4194304 | tf_op jit(solution)/shard_map/reshape | solution.py:58
  18.7 3.6 %all-to-all-start.1 = ((bf16[256,32,128]{2,0,1:T(8,128)(2,1)}), bf16[256,32,128]{2,0,1:T(8,128)(2,1)S(1)}, u32[]{:S(2)}, u32[]{:S(2)}) async-start(bf16[256,32,128]{2,0,1:T(8,128)(2,1)} %copy.45), calls=%async_computation.1 | async-start | bytes 4194304 | tf_op jit(solution)/shard_map/all_to_all | solution.py:62
  22.5 1.3 multiply_convert_fusion.2
  23.8 3.8 %pad_maximum_fusion = bf16[1024,8,273]{0,2,1:T(8,128)(2,1)} fusion(bf16[1024,8,256]{0,2,1:T(8,128)(2,1)S(1)} %bitcast.82, bf16[1024,8,16]{0,2,1:T(8,128)(2,1)S(1)} %multiply_convert_fusion.3, bf16[273]{0:T(512)(128)(2,1)S(1)} %pad.11.clone), kind=kLoop, calls=%fused_computation.67 | loop fusion | flops 13418496 | bytes 8929826 | tf_op jit(solution)/shard_map/concatenate | solution.py:51
  27.6 20.3 %all-to-all-done.1 = bf16[256,32,128]{2,0,1:T(8,128)(2,1)S(1)} async-done(((bf16[256,32,128]{2,0,1:T(8,128)(2,1)}), bf16[256,32,128]{2,0,1:T(8,128)(2,1)S(1)}, u32[]{:S(2)}, u32[]{:S(2)}) %all-to-all-start.1) | async-done | bytes 2097184 | tf_op jit(solution)/shard_map/all_to_all | solution.py:62
  48.0 1.3 copy-done.2
  49.3 1.7 copy.47
  51.0 4.4 %fusion.77 = f32[8,273,128]{2,1,0:T(8,128)S(1)} fusion(bf16[1024,8,273]{0,2,1:T(8,128)(2,1)} %pad_maximum_fusion, bf16[1024,8,128]{2,0,1:T(8,128)(2,1)S(1)} %bitcast.77), kind=kOutput, calls=%fused_computation.87 | convolution fusion | flops 572522496 | bytes 7688192 | tf_op jit(solution)/shard_map/bhf,bhv->hfv/dot_general | solution.py:75
  55.5 1.2 copy.48
  56.7 0.8 copy.50
  57.6 3.4 %all-to-all-start.2 = ((bf16[256,32,16]{0,2,1:T(8,128)(2,1)}), bf16[256,32,16]{0,2,1:T(8,128)(2,1)S(1)}, u32[]{:S(2)}, u32[]{:S(2)}) async-start(bf16[256,32,16]{0,2,1:T(8,128)(2,1)} %bitcast.17), calls=%async_computation.2 | async-start | bytes 524288 | tf_op jit(solution)/shard_map/all_to_all | solution.py:60
  61.0 0.7 slice.11
  61.7 4.1 %collective-permute-start.1 = (bf16[64,8,16]{0,2,1:T(8,128)(2,1)}, bf16[64,8,16]{0,2,1:T(8,128)(2,1)S(1)}, u32[]{:S(2)}, u32[]{:S(2)}) collective-permute-start(bf16[64,8,16]{0,2,1:T(8,128)(2,1)} %slice.11), channel_id=1, source_target_pairs={{0,4},{4,8},{8,12},{1,5},{5,9},{9,13},{2,6},{6,10},{10,14},{3,7},{... | collective-permute-start | bytes 49160 | tf_op jit(solution)/shard_map/ppermute | solution.py:29
  65.9 1.1 all-to-all-done.2
  67.0 0.7 copy-done.4
  67.7 1.0 copy.65
  68.7 4.3 %collective-permute-start = (bf16[64,8,128]{2,0,1:T(8,128)(2,1)S(1)}, bf16[64,8,128]{2,0,1:T(8,128)(2,1)S(1)}, u32[]{:S(2)}, u32[]{:S(2)}) collective-permute-start(bf16[64,8,128]{2,0,1:T(8,128)(2,1)S(1)} %slice.10), channel_id=1, source_target_pairs={{0,4},{4,8},{8,12},{1,5},{5,9},{9,13},{2,6},{6,10},{10,14},{3,7},{... | collective-permute-start | bytes 393224 | tf_op jit(solution)/shard_map/ppermute | solution.py:29
  73.1 1.8 pad_maximum_fusion.3
  74.9 4.2 %collective-permute-done = bf16[64,8,128]{2,0,1:T(8,128)(2,1)S(1)} collective-permute-done((bf16[64,8,128]{2,0,1:T(8,128)(2,1)S(1)}, bf16[64,8,128]{2,0,1:T(8,128)(2,1)S(1)}, u32[]{:S(2)}, u32[]{:S(2)}) %collective-permute-start) | collective-permute-done | bytes 131104 | tf_op jit(solution)/shard_map/ppermute | solution.py:29
  79.0 1.5 pad_maximum_fusion.1
  80.6 67.5 %all-gather.3.cloned.1.call-done = f32[32,273,128]{2,0,1:T(8,128)} async-done(((f32[8,273,128]{2,0,1:T(8,128)}), f32[32,273,128]{2,0,1:T(8,128)}) %all-gather.3.cloned.1.call-update) | async-done | bytes 4472848 | tf_op jit(solution)/shard_map/all_gather | solution.py:34
  148.1 7.5 %while.32 = (s32[]{:T(128)}, f32[8,273,128]{2,1,0:T(8,128)S(1)}, s32[]{:T(128)}, f32[4,8,273,128]{3,1,0,2:T(8,128)}, s32[]{:T(128)}, /*index=5*/s32[]{:T(128)}) while((s32[]{:T(128)}, f32[8,273,128]{2,1,0:T(8,128)S(1)}, s32[]{:T(128)}, f32[4,8,273,128]{3,1,0,2:T(8,128)}, s32[]{:T(128)}, /*index=5*/s32[]{:T(128)}) %tuple.74), condition=%wide.region_1.2_spmd.clone, body=%wide.region_0.1_spmd.clone.sunk | while | flops 838660 | bytes 5591141 | solution.py:42
  148.1 1.3 constant_dynamic-slice_fusion.3
  149.4 0.5 add_select_fusion.2
  149.9 1.3 constant_dynamic-slice_fusion.3
  151.3 0.5 add_select_fusion.2
  151.8 1.3 constant_dynamic-slice_fusion.3
  153.2 0.5 add_select_fusion.2
  153.7 1.3 constant_dynamic-slice_fusion.3
  155.1 0.5 add_select_fusion.2
  155.6 57.8 %while.31 = (s32[]{:T(128)}, f32[8,273,128]{2,1,0:T(8,128)S(1)}, f32[2,512,8,128]{1,3,2,0:T(8,128)}, f32[2,512,8,128]{3,2,1,0:T(8,128)}, s32[2]{0:T(128)S(1)}, /...) while((s32[]{:T(128)}, f32[8,273,128]{2,1,0:T(8,128)S(1)}, ...), condition=%wide.region_5.6_spmd, body=%wide.region_2.5_spmd.sunk | while | flops 1977677568 | bytes 75423312 | solution.py:131
  155.6 0.8 iota_compare_fusion.3
  156.5 0.6 dynamic_slice.146
  157.7 4.5 %fusion.111 = f32[8,128,512]{2,1,0:T(8,128)S(1)} fusion(pred[512,512]{1,0:T(8,128)(4,1)} %iota_compare_fusion.3, bf16[1024,8,128]{2,0,1:T(8,128)(2,1)} %get-tuple-element.499, s32[]{:T(128)S(6)} %select_n.151, bf16[1024,8,16]{0,2,1:T(8,128)(2,1)} %get-tuple-element.501, bf16[1024,8,16]{0,2,1:T(8,128)(2,1)S(1)} %get-tuple-element.500), kind=kOutput, calls=%fused_computation.13.clone.1 | convolution fusion | flops 618659840 | bytes 3671552 | tf_op jit(solution)/shard_map/while/body/eval_jaxpr/hbc,chv->bhv/dot_general | solution.py:101
  162.3 0.7 multiply_convert_fusion.6
  163.0 2.5 bitcast_dynamic-update-slice_fusion.2
  165.6 1.0 fusion.110
  167.0 7.4 %fusion.114 = (f32[8,512]{1,0:T(8,128)S(1)}, f32[8,512,576]{1,2,0:T(8,128)}) fusion(pred[512,576]{0,1:T(8,128)(4,1)S(1)} %fusion.113, bf16[1088,8,16]{0,2,1:T(8,128)(2,1)S(1)} %copy-done.5, s32[]{:T(128)S(6)} %select_n.152, bf16[1024,8,16]{0,2,1:T(8,128)(2,1)S(1)} %get-tuple-element.500, s32[]{:T(128)S(6)} %select_n.151), kind=kOutput, calls=%fused_computation.86.clone.1 | convolution fusion | flops 165151296 | bytes 10635264 | tf_op jit(solution)/shard_map/while/body/eval_jaxpr/sub | solution.py:124
  174.4 6.5 %fusion.115 = f32[1,512,8,128]{1,3,2,0:T(8,128)} fusion(f32[8,512,576]{1,2,0:T(8,128)} %get-tuple-element.431, f32[8,512]{1,0:T(8,128)S(1)} %get-tuple-element.432, bf16[1088,8,128]{2,0,1:T(8,128)(2,1)} %get-tuple-element.502, s32[]{:T(128)S(6)} %select_n.152), kind=kOutput, calls=%fused_computation.25.clone.1 | convolution fusion | flops 608698368 | bytes 12730372 | tf_op jit(solution)/shard_map/while/body/eval_jaxpr/hbc,chv->bhv/dot_general | solution.py:126
  180.9 2.1 copy.71
  183.0 1.5 constant_dynamic-update-slice_fusion.2
  184.5 0.8 iota_compare_fusion.3
  185.3 0.6 dynamic_slice.146
  186.6 4.5 %fusion.111 = f32[8,128,512]{2,1,0:T(8,128)S(1)} fusion(pred[512,512]{1,0:T(8,128)(4,1)} %iota_compare_fusion.3, bf16[1024,8,128]{2,0,1:T(8,128)(2,1)} %get-tuple-element.499, s32[]{:T(128)S(6)} %select_n.151, bf16[1024,8,16]{0,2,1:T(8,128)(2,1)} %get-tuple-element.501, bf16[1024,8,16]{0,2,1:T(8,128)(2,1)S(1)} %get-tuple-element.500), kind=kOutput, calls=%fused_computation.13.clone.1 | convolution fusion | flops 618659840 | bytes 3671552 | tf_op jit(solution)/shard_map/while/body/eval_jaxpr/hbc,chv->bhv/dot_general | solution.py:101
  191.2 0.7 multiply_convert_fusion.6
  191.9 2.5 bitcast_dynamic-update-slice_fusion.2
  194.4 1.0 fusion.110
  195.9 7.4 %fusion.114 = (f32[8,512]{1,0:T(8,128)S(1)}, f32[8,512,576]{1,2,0:T(8,128)}) fusion(pred[512,576]{0,1:T(8,128)(4,1)S(1)} %fusion.113, bf16[1088,8,16]{0,2,1:T(8,128)(2,1)S(1)} %copy-done.5, s32[]{:T(128)S(6)} %select_n.152, bf16[1024,8,16]{0,2,1:T(8,128)(2,1)S(1)} %get-tuple-element.500, s32[]{:T(128)S(6)} %select_n.151), kind=kOutput, calls=%fused_computation.86.clone.1 | convolution fusion | flops 165151296 | bytes 10635264 | tf_op jit(solution)/shard_map/while/body/eval_jaxpr/sub | solution.py:124
  203.3 6.5 %fusion.115 = f32[1,512,8,128]{1,3,2,0:T(8,128)} fusion(f32[8,512,576]{1,2,0:T(8,128)} %get-tuple-element.431, f32[8,512]{1,0:T(8,128)S(1)} %get-tuple-element.432, bf16[1088,8,128]{2,0,1:T(8,128)(2,1)} %get-tuple-element.502, s32[]{:T(128)S(6)} %select_n.152), kind=kOutput, calls=%fused_computation.25.clone.1 | convolution fusion | flops 608698368 | bytes 12730372 | tf_op jit(solution)/shard_map/while/body/eval_jaxpr/hbc,chv->bhv/dot_general | solution.py:126
  209.9 2.1 copy.71
  212.0 1.5 constant_dynamic-update-slice_fusion.2
  213.4 5.2 %copy.52 = f32[2,512,8,128]{3,2,1,0:T(8,128)} copy(f32[2,512,8,128]{1,3,2,0:T(8,128)} %get-tuple-element.272) | data formatting | bytes 8388608 | tf_op jit(solution)/shard_map/while | solution.py:131
  218.7 2.8 %multiply_reduce_fusion = f32[2,512,8]{1,2,0:T(8,128)S(1)} fusion(f32[2,512,8,128]{1,3,2,0:T(8,128)} %get-tuple-element.272), kind=kLoop, calls=%fused_computation.69 | loop fusion | flops 2088960 | bytes 4227072 | tf_op jit(solution)/shard_map/reduce_sum | solution.py:134
  221.7 4.1 %add_convert_fusion = bf16[4,256,8,128]{3,2,1,0:T(8,128)(2,1)S(1)} fusion(f32[4,256,8,128]{3,2,1,0:T(8,128)} %bitcast.94, f32[4,256,8,128]{3,2,1,0:T(8,128)} %bitcast.81, f32[8,128]{1,0:T(8,128)S(1)} %bitcast.101, f32[4,256,8]{2,1,0:T(8,128)S(1)} %copy.53), kind=kLoop, calls=%fused_computation.68 | loop fusion | flops 4194304 | bytes 10522624 | tf_op jit(solution)/shard_map/convert_element_type | solution.py:136
  226.0 1.4 collective-permute-start.4
  227.3 0.4 collective-permute-start.3
  227.9 11.7 %collective-permute-done.4 = bf16[256,8,128]{2,1,0:T(8,128)(2,1)S(1)} collective-permute-done((bf16[256,8,128]{2,1,0:T(8,128)(2,1)S(1)}, bf16[256,8,128]{2,1,0:T(8,128)(2,1)S(1)}, u32[]{:S(2)}, u32[]{:S(2)}) %collective-permute-start.4) | collective-permute-done | bytes 524320 | tf_op jit(solution)/shard_map/ppermute | solution.py:143
  239.6 12.0 %collective-permute-done.3 = bf16[256,8,128]{2,1,0:T(8,128)(2,1)S(1)} collective-permute-done((bf16[256,8,128]{2,1,0:T(8,128)(2,1)S(1)}, bf16[256,8,128]{2,1,0:T(8,128)(2,1)S(1)}, u32[]{:S(2)}, u32[]{:S(2)}) %collective-permute-start.3) | collective-permute-done | bytes 524320 | tf_op jit(solution)/shard_map/ppermute | solution.py:143
  251.9 2.1 gather_fusion
  254.0 3.0 %copy.55 = bf16[256,4,8,128]{0,3,2,1:T(8,128)(2,1)S(1)} copy(bf16[256,4,8,128]{3,2,0,1:T(8,128)(2,1)} %bitcast.85) | data formatting | bytes 4194304 | tf_op jit(solution)/shard_map/transpose | solution.py:23
  257.0 2.9 %copy.56 = bf16[256,4096]{1,0:T(8,128)(2,1)} copy(bf16[256,4096]{0,1:T(8,128)(2,1)S(1)} %bitcast.86) | data formatting | bytes 4194304 | tf_op jit(solution)/shard_map/reshape;reshape | solution.py:147
  (63 shorter events, 1.9 us)
Async XLA Ops:
  8.3 10.3 %all-to-all-start = ((bf16[256,32,16]{0,2,1:T(8,128)(2,1)}), bf16[256,32,16]{0,2,1:T(8,128)(2,1)S(1)}, u32[]{:S(2)}, u32[]{:S(2)}) async-start(bf16[256,32,16]{0,2,1:T(8,128)(2,1)} %bitcast.7), calls=%async_computation | async-start | bytes 524288 | tf_op jit(solution)/shard_map/all_to_all | solution.py:61
  18.7 29.3 %all-to-all-start.1 = ((bf16[256,32,128]{2,0,1:T(8,128)(2,1)}), bf16[256,32,128]{2,0,1:T(8,128)(2,1)S(1)}, u32[]{:S(2)}, u32[]{:S(2)}) async-start(bf16[256,32,128]{2,0,1:T(8,128)(2,1)} %copy.45), calls=%async_computation.1 | async-start | bytes 4194304 | tf_op jit(solution)/shard_map/all_to_all | solution.py:62
  22.3 125.8 %all-gather.3.cloned.1.call-start = ((), (), s32[]{:S(2)}) async-start(), calls=%async_computation.3 | async-start | bytes 5591040 | tf_op jit(solution)/shard_map/all_gather | solution.py:34
  22.4 38.6 %copy-start.3 = (bf16[4,8,2,8,256]{4,3,0,2,1:T(8,128)(2,1)}, bf16[4,8,2,8,256]{4,3,0,2,1:T(8,128)(2,1)S(1)}, u32[]{:S(2)}) copy-start(bf16[4,8,2,8,256]{4,3,0,2,1:T(8,128)(2,1)S(1)} %copy.64) | copy-start | bytes 786436
  48.0 1.3 copy-start.2
  51.0 28.0 %copy-start = (bf16[4,256,8,128]{3,1,0,2:T(8,128)(2,1)}, bf16[4,256,8,128]{3,1,0,2:T(8,128)(2,1)S(1)}, u32[]{:S(2)}) copy-start(bf16[4,256,8,128]{3,1,0,2:T(8,128)(2,1)S(1)} %copy.47) | copy-start | bytes 6291460
  51.0 5.7 %copy-start.6 = (bf16[256,512]{1,0:T(8,128)(2,1)S(1)}, bf16[256,512]{1,0:T(8,128)(2,1)}, u32[]{:S(2)}) copy-start(bf16[256,512]{1,0:T(8,128)(2,1)} %param.8) | copy-start | bytes 786436
  57.6 9.4 %all-to-all-start.2 = ((bf16[256,32,16]{0,2,1:T(8,128)(2,1)}), bf16[256,32,16]{0,2,1:T(8,128)(2,1)S(1)}, u32[]{:S(2)}, u32[]{:S(2)}) async-start(bf16[256,32,16]{0,2,1:T(8,128)(2,1)} %bitcast.17), calls=%async_computation.2 | async-start | bytes 524288 | tf_op jit(solution)/shard_map/all_to_all | solution.py:60
  61.7 11.4 %collective-permute-start.1 = (bf16[64,8,16]{0,2,1:T(8,128)(2,1)}, bf16[64,8,16]{0,2,1:T(8,128)(2,1)S(1)}, u32[]{:S(2)}, u32[]{:S(2)}) collective-permute-start(bf16[64,8,16]{0,2,1:T(8,128)(2,1)} %slice.11), channel_id=1, source_target_pairs={{0,4},{4,8},{8,12},{1,5},{5,9},{9,13},{2,6},{6,10},{10,14},{3,7},{... | collective-permute-start | bytes 49160 | tf_op jit(solution)/shard_map/ppermute | solution.py:29
  67.0 0.7 copy-start.4
  68.7 10.3 %collective-permute-start = (bf16[64,8,128]{2,0,1:T(8,128)(2,1)S(1)}, bf16[64,8,128]{2,0,1:T(8,128)(2,1)S(1)}, u32[]{:S(2)}, u32[]{:S(2)}) collective-permute-start(bf16[64,8,128]{2,0,1:T(8,128)(2,1)S(1)} %slice.10), channel_id=1, source_target_pairs={{0,4},{4,8},{8,12},{1,5},{5,9},{9,13},{2,6},{6,10},{10,14},{3,7},{... | collective-permute-start | bytes 393224 | tf_op jit(solution)/shard_map/ppermute | solution.py:29
  162.3 3.3 %slice-start = ((s8[4587520]{0:T(1024)(128)(4,1)}), s8[4194304]{0:T(1024)(128)(4,1)S(1)}, s32[]{:S(2)}) async-start(s8[4587520]{0:T(1024)(128)(4,1)} %bitcast.75), calls=%async_computation.4 | async-start | bytes 8388608 | tf_op jit(solution)/shard_map/while
  163.0 2.6 copy-start.1
  163.0 2.5 slice-start.1
  165.5 1.4 copy-start.5
  191.2 3.3 %slice-start = ((s8[4587520]{0:T(1024)(128)(4,1)}), s8[4194304]{0:T(1024)(128)(4,1)S(1)}, s32[]{:S(2)}) async-start(s8[4587520]{0:T(1024)(128)(4,1)} %bitcast.75), calls=%async_computation.4 | async-start | bytes 8388608 | tf_op jit(solution)/shard_map/while
  191.8 2.6 copy-start.1
  191.9 2.5 slice-start.1
  194.4 1.5 copy-start.5
  218.7 3.0 %copy-start.7 = (f32[1024]{0:T(1024)S(1)}, f32[1024]{0:T(1024)}, u32[]{:S(2)}) copy-start(f32[1024]{0:T(1024)} %param.11) | copy-start | bytes 12292
  226.0 13.7 %collective-permute-start.4 = (bf16[256,8,128]{2,1,0:T(8,128)(2,1)S(1)}, bf16[256,8,128]{2,1,0:T(8,128)(2,1)S(1)}, u32[]{:S(2)}, u32[]{:S(2)}) collective-permute-start(bf16[256,8,128]{2,1,0:T(8,128)(2,1)S(1)} %get-tuple-element.332), channel_id=1, source_target_pairs={{0,3},{1,0},{2,1},{3,2},{4,7},{5,4},{6,5},{7,6},{8,11},{9,8},{10,9... | collective-permute-start | bytes 1572872 | tf_op jit(solution)/shard_map/ppermute | solution.py:143
  227.3 24.3 %collective-permute-start.3 = (bf16[256,8,128]{2,1,0:T(8,128)(2,1)S(1)}, bf16[256,8,128]{2,1,0:T(8,128)(2,1)S(1)}, u32[]{:S(2)}, u32[]{:S(2)}) collective-permute-start(bf16[256,8,128]{2,1,0:T(8,128)(2,1)S(1)} %get-tuple-element.333), channel_id=1, source_target_pairs={{0,2},{1,3},{2,0},{3,1},{4,6},{5,7},{6,4},{7,5},{8,10},{9,11},{10,... | collective-permute-start | bytes 1572872 | tf_op jit(solution)/shard_map/ppermute | solution.py:143
  227.7 23.8 %collective-permute-start.2 = (bf16[256,8,128]{2,1,0:T(8,128)(2,1)S(1)}, bf16[256,8,128]{2,1,0:T(8,128)(2,1)S(1)}, u32[]{:S(2)}, u32[]{:S(2)}) collective-permute-start(bf16[256,8,128]{2,1,0:T(8,128)(2,1)S(1)} %get-tuple-element.334), channel_id=1, source_target_pairs={{0,1},{1,2},{2,3},{3,0},{4,5},{5,6},{6,7},{7,4},{8,9},{9,10},{10,1... | collective-permute-start | bytes 1572872 | tf_op jit(solution)/shard_map/ppermute | solution.py:143
Sparse Core Ops, SparseCore 0:
  56.8 91.1 all-gather.2
